TPU v7x, 128 devices: a whole 4x4x4 slice. The times are simulated.
128 devices in a mesh: dp: 4 (over z), tensor: 32 (over x, y, core).
Axes of the slice: x: 4, y: 4, z: 4, core: 2. Of those that a mesh axis runs over, the one named last changes fastest.
Arguments:
- tokens: bfloat16 [4, 1536, 4096], P('dp', 'tensor'), may hold values from -6 to 6
- ln_gain: float32 [4096], replicated, may hold values from 0.1 to 1.9
- ln_bias: float32 [4096], replicated, may hold values from -3 to 3
- w_qkv: bfloat16 [4096, 3, 4096], P(None, None, 'tensor'), may hold values from -0.375 to 0.375
- w_out: bfloat16 [4096, 4096], P(None, 'tensor'), may hold values from -0.09375 to 0.09375
- layer_scale: float32 [4096], P('tensor'), may hold values from 0.5 to 4
- w_merge: bfloat16 [4, 4096, 4096], P(None, 'tensor'), may hold values from -0.046875 to 0.046875
- segment_ids: int32 [4, 1536], P('dp'), may hold values from 0 to 3, as said below
- grid_sizes: int32 [4, 3, 2], P('dp'), may hold values from 14 to 28, as said below
- owners: int32 [4, 384, 1], P('dp'), may hold values from 0 to 127; in each aligned block of 384 rows (0 to 383, 384 to 767, ..., all dimensions but the last counted through in order) at most 4 rows name the same one
Outputs:
- received: bfloat16 [4, 512, 4096], P('dp', 'tensor')
Inputs may be any that keep to these rules, and one draw needn't show every extreme that they name: `grid_sizes`: both sides of every grid are even; in every batch one image has sides 28 x 28 and the others have sides of at most 18. `segment_ids`: the images of a batch lie end to end from slot 0 in order; the 5 + h w slots of image i hold i, and the padding after the last image holds 3. `owners`: within one batch no owner is named by more than 4 rows, a bound that some block reaches.
All inputs are finite; a program needn't handle non-finite values.
Results may differ from a plain program's by a relative error of at most 0.01.
Values may be sent and summed in bfloat16 or wider, within the bound.
No kernel may reach another device: no remote copies, remote signals or barrier semaphores. Data moves between devices by JAX's collectives and lax.ppermute only.
A program may use at most 128 MiB of HBM per device.

v0:
```python
import jax
import jax.numpy as jnp
from jax import lax
from jax.sharding import PartitionSpec as P

HEAD_DIM = 128
IMGS = 3
REG = 5


norm_eps = 1e-06


def layer_norm(row_data, gain_vec, shift_vec):
    values = row_data.astype(jnp.float32)
    center = values - jnp.mean(values, axis=-1, keepdims=True)
    spread = jnp.mean(center * center, axis=-1, keepdims=True)
    return (center * lax.rsqrt(spread + norm_eps) * gain_vec + shift_vec).astype(jnp.bfloat16)


def image_layout(grid_row):
    heights = grid_row[:, 0]
    widths = grid_row[:, 1]
    lengths = REG + heights * widths
    starts = jnp.cumsum(lengths) - lengths
    counts = heights // 2 * (widths // 2)
    merged_end = jnp.cumsum(counts)
    return (heights, widths, starts, merged_end - counts, merged_end)


def pick_rows(onehot, lookup):
    return jnp.sum(onehot * lookup[None, :], axis=1)


def rope_tables(seg_row, grid_row, seq_len):
    heights, widths, starts, first_merged, last_merged = image_layout(grid_row)
    position = jnp.arange(seq_len, dtype=jnp.int32)
    image_ids = jnp.arange(IMGS, dtype=jnp.int32)
    onehot = (seg_row[:, None] == image_ids[None, :]).astype(jnp.int32)
    is_image = jnp.sum(onehot, axis=1) > 0
    in_image = position - pick_rows(onehot, starts) - REG
    is_patch = is_image & (in_image >= 0)
    row_width = jnp.maximum(pick_rows(onehot, widths), 1)
    col_height = jnp.maximum(pick_rows(onehot, heights), 1)
    clipped = jnp.maximum(in_image, 0)
    coord_y = (
        2.0 * ((clipped // row_width).astype(jnp.float32) + 0.5) / col_height.astype(jnp.float32)
        - 1.0
    )
    coord_x = (
        2.0 * ((clipped % row_width).astype(jnp.float32) + 0.5) / row_width.astype(jnp.float32)
        - 1.0
    )
    quarter = HEAD_DIM // 4
    pair_ids = jnp.arange(HEAD_DIM // 2, dtype=jnp.int32)
    omegas = 100.0 ** ((pair_ids % quarter).astype(jnp.float32) / quarter)
    coord_all = jnp.where(pair_ids[None, :] < quarter, coord_y[:, None], coord_x[:, None])
    angles = jnp.where(is_patch[:, None], jnp.pi * omegas[None, :] * coord_all, 0.0)
    return (jnp.cos(angles), jnp.sin(angles))


def rotate(values, cos_rows, sin_rows):
    half_dim = values.shape[-1] // 2
    first_half = values[..., :half_dim]
    second_half = values[..., half_dim:]
    return jnp.concatenate(
        [
            first_half * cos_rows - second_half * sin_rows,
            second_half * cos_rows + first_half * sin_rows,
        ],
        axis=-1,
    )


def merge_sources(grid_row, merged_rows):
    heights, widths, starts, first_merged, last_merged = image_layout(grid_row)
    row_ids = jnp.arange(merged_rows, dtype=jnp.int32)
    onehot = (
        (row_ids[:, None] >= first_merged[None, :]) & (row_ids[:, None] < last_merged[None, :])
    ).astype(jnp.int32)
    is_valid = jnp.sum(onehot, axis=1) > 0
    row_width = pick_rows(onehot, widths)
    half_width = jnp.maximum(row_width // 2, 1)
    in_image = row_ids - pick_rows(onehot, first_merged)
    corner = (
        pick_rows(onehot, starts)
        + REG
        + 2 * (in_image // half_width) * row_width
        + 2 * (in_image % half_width)
    )
    offsets = jnp.stack(
        [jnp.zeros_like(row_width), jnp.ones_like(row_width), row_width, row_width + 1], axis=1
    )
    sources = jnp.where(is_valid[:, None], corner[:, None] + offsets, 0)
    return (sources, is_valid)


def attend(query_rows, query_seg, key_rows, value_rows, key_seg):
    scores = lax.dot_general(
        query_rows, key_rows, (((1,), (1,)), ((), ())), preferred_element_type=jnp.float32
    ) * HEAD_DIM ** (-0.5)
    scores = jnp.where(query_seg[:, None] == key_seg[None, :], scores, -jnp.inf)
    shifted = jnp.exp(scores - jnp.max(scores, axis=1, keepdims=True))
    weights = (shifted / jnp.sum(shifted, axis=1, keepdims=True)).astype(jnp.bfloat16)
    return jnp.dot(weights, value_rows, preferred_element_type=jnp.float32).astype(jnp.bfloat16)


def owner_ranks(owner_row, device_count):
    onehot = (owner_row[:, None] == jnp.arange(device_count, dtype=jnp.int32)[None, :]).astype(
        jnp.int32
    )
    before = jnp.cumsum(onehot, axis=0) - onehot
    return jnp.sum(before * onehot, axis=1)


def local(
    tokens, ln_gain, ln_bias, w_qkv, w_out, layer_scale, w_merge, segment_ids, grid_sizes, owners
):
    tensor_count = lax.axis_size("tensor")
    batch_count = lax.axis_size("dp")
    seg_row = segment_ids[0]
    grid_row = grid_sizes[0]
    owner_row = owners[0, :, 0]
    seq_len = seg_row.shape[0]
    model_width = tokens.shape[2]
    col_width = layer_scale.shape[0]
    head_width = w_qkv.shape[2]
    local_heads = head_width // HEAD_DIM
    merged_rows = seq_len // 4
    device_count = batch_count * tensor_count
    own_cap = max(2, 3 * merged_rows // (2 * device_count))
    out_width = w_merge.shape[2]
    cos_table, sin_table = rope_tables(seg_row, grid_row, seq_len)
    qkv_weight = w_qkv.reshape(model_width, 3 * head_width)
    normed_local = layer_norm(tokens[0], ln_gain, ln_bias)[None]
    normed = lax.all_gather(normed_local, "tensor", axis=1, tiled=True)[0]
    count_rows = normed.shape[0]
    product = jnp.dot(normed, qkv_weight, preferred_element_type=jnp.float32)
    cos_rows = cos_table[:, None, :]
    sin_rows = sin_table[:, None, :]
    query_part = rotate(
        product[:, :head_width].reshape(count_rows, local_heads, HEAD_DIM), cos_rows, sin_rows
    ).reshape(count_rows, head_width)
    key_part = rotate(
        product[:, head_width : 2 * head_width].reshape(count_rows, local_heads, HEAD_DIM),
        cos_rows,
        sin_rows,
    ).reshape(count_rows, head_width)
    qkv_rows = jnp.concatenate([query_part, key_part, product[:, 2 * head_width :]], axis=1).astype(
        jnp.bfloat16
    )[None][0]
    input_cols = lax.all_to_all(tokens, "tensor", split_axis=2, concat_axis=1, tiled=True)[0]
    block_len = min(512, seq_len)
    block_count = seq_len // block_len
    query_rows = qkv_rows[:, 0:HEAD_DIM]
    key_rows = qkv_rows[:, head_width : head_width + HEAD_DIM]
    value_rows = qkv_rows[:, 2 * head_width : 2 * head_width + HEAD_DIM]

    def one_block(block_index):
        first_row = block_index * block_len
        query_block = lax.dynamic_slice_in_dim(query_rows, first_row, block_len, 0)
        seg_block = lax.dynamic_slice_in_dim(seg_row, first_row, block_len, 0)
        return attend(query_block, seg_block, key_rows, value_rows, seg_row)

    head_outputs = lax.map(one_block, jnp.arange(block_count, dtype=jnp.int32)).reshape(
        seq_len, HEAD_DIM
    )
    mixed = jnp.dot(
        lax.all_gather(head_outputs, "tensor", axis=1, tiled=True),
        w_out,
        preferred_element_type=jnp.float32,
    )
    hidden = (input_cols.astype(jnp.float32) + layer_scale * mixed).astype(jnp.bfloat16)
    sources, is_valid = merge_sources(grid_row, merged_rows)
    merged = jnp.where(
        is_valid[:, None, None], hidden[sources], jnp.zeros((), jnp.bfloat16)
    ).reshape(merged_rows, 4 * col_width)
    merge_weight = w_merge.reshape(4 * col_width, out_width)
    ranks = owner_ranks(owner_row, device_count)
    slot_keys = owner_row * own_cap + ranks
    slot_ids = jnp.arange(device_count * own_cap, dtype=jnp.int32)
    placing = (slot_ids[:, None] == slot_keys[None, :]).astype(jnp.bfloat16)
    by_owner = jnp.dot(placing, merged, preferred_element_type=jnp.float32).astype(jnp.bfloat16)
    group_part = jnp.dot(by_owner, merge_weight, preferred_element_type=jnp.float32).astype(
        jnp.bfloat16
    )
    outgoing = group_part.reshape(device_count, own_cap, out_width)
    incoming = lax.all_to_all(outgoing, ("dp", "tensor"), split_axis=0, concat_axis=0, tiled=True)
    arrived = jnp.sum(
        incoming.reshape(batch_count, tensor_count, own_cap, out_width).astype(jnp.float32), axis=1
    )
    return arrived.astype(jnp.bfloat16).reshape(1, batch_count * own_cap, out_width)


def solution(mesh):
    in_specs = (
        P("dp", "tensor", None),
        P(),
        P(),
        P(None, None, "tensor"),
        P(None, "tensor"),
        P("tensor"),
        P(None, "tensor", None),
        P("dp", None),
        P("dp", None, None),
        P("dp", None, None),
    )
    out_specs = P("dp", "tensor", None)
    return jax.shard_map(local, mesh=mesh, in_specs=in_specs, out_specs=out_specs, check_vma=False)
```

profile of v0, /device:TPU:1, one launch (start us, length us, event | category | flops | bytes accessed | tf_op | source)
XLA Modules:
  0.0 268.0 jit_solution(14367881695849140049)
XLA Ops:
  6.5 1.2 convert_reduce_fusion
  7.8 1.3 fusion.18
  9.1 2.0 fusion.15
  11.1 0.0 all-gather.5.cloned.1.call-start
  11.2 0.8 fusion.59
  11.9 0.2 reduce-window.27
  12.1 0.2 reduce-window.28
  12.3 0.7 reduce.5
  13.0 4.7 %copy.37 = bf16[4096,3,128]{0,2,1:T(8,128)(2,1)} copy(bf16[4096,3,128]{2,0,1:T(8,128)(2,1)} %param.15) | data formatting | bytes 6291456 | tf_op args[3]
  17.8 0.5 multiply_subtract_fusion
  18.3 0.1 convert_reduce_fusion.1
  18.4 0.2 fusion.38
  18.6 58.9 %all-gather.3.cloned.1.call-done = bf16[1,1536,4096]{2,1,0:T(8,128)(2,1)} async-done(((bf16[1,48,4096]{2,1,0:T(8,128)(2,1)}), bf16[1,1536,4096]{2,1,0:T(8,128)(2,1)}) %all-gather.3.cloned.1.call-update) | async-done | bytes 12582928 | tf_op jit(solution)/shard_map/all_gather | solution.py:136
  77.5 9.0 %fusion.8 = f32[1536,384]{0,1:T(8,128)S(1)} fusion(bf16[4096,384]{0,1:T(8,128)(2,1)} %bitcast.85, bf16[1,1536,4096]{2,1,0:T(8,128)(2,1)} %all-gather.3.cloned.1.call-done), kind=kOutput, calls=%fused_computation.12 | convolution fusion | flops 4831838208 | bytes 18087936 | tf_op jit(solution)/shard_map/dot_general | solution.py:138
  86.6 0.1 slice_bitcast_fusion
  86.7 1.8 subtract_convert_fusion
  88.5 0.1 maximum_bitcast_fusion
  88.6 0.2 copy.39
  88.8 0.2 copy.40
  89.1 11.1 %while.10 = (s32[]{:T(128)}, bf16[3,512,128]{2,1,0:T(8,128)(2,1)S(1)}, s32[3]{0:T(128)S(1)}, s32[1536]{0:T(1024)S(1)}, s32[1,1536]{1,0:T(1,128)S(1)}, /*index=5*...) while((s32[]{:T(128)}, ...), condition=%wide.region_15.16_spmd, body=%wide.region_12.15_spmd.sunk | while | flops 409795584 | bytes 10522815 | solution.py:165
  89.1 0.7 dynamic_slice.18
  90.5 0.1 dynamic_slice.19
  90.6 0.9 fusion.76
  91.4 0.6 fusion.77
  92.0 0.8 fusion.78
  92.8 0.7 dynamic_slice.18
  94.2 0.1 dynamic_slice.19
  94.3 0.9 fusion.76
  95.1 0.6 fusion.77
  95.7 0.8 fusion.78
  96.5 0.7 dynamic_slice.18
  97.8 0.1 dynamic_slice.19
  97.9 0.9 fusion.76
  98.8 0.6 fusion.77
  99.4 0.8 fusion.78
  100.2 0.8 copy-done.2
  101.0 2.8 %copy.35 = bf16[1,48,4096]{1,0,2:T(2,128)(2,1)S(1)} copy(bf16[1,48,4096]{2,1,0:T(8,128)(2,1)S(1)} %copy-done.1) | data formatting | bytes 786432 | tf_op args[0]
  103.8 0.5 broadcast.721
  104.3 23.6 %reduce.6 = bf16[4096,48]{1,0:T(8,128)(2,1)} reduce(bf16[4096,1,48]{2,1,0:T(2,128)(2,1)S(1)} %bitcast.83, bf16[]{:T(256)} %broadcast.721), dimensions={1}, to_apply=%bitcast.65.reduce_sub_computation | reduce | bytes 786434
  128.0 3.8 %reshape.688 = bf16[32,2,3072]{2,1,0:T(2,128)(2,1)} reshape(bf16[4096,48]{1,0:T(8,128)(2,1)} %reduce.6) | data formatting | bytes 786432
  131.7 5.4 %all-to-all-start = ((bf16[32,2,3072]{2,1,0:T(2,128)(2,1)}), bf16[32,2,3072]{2,1,0:T(2,128)(2,1)S(1)}, u32[]{:S(2)}, u32[]{:S(2)}) async-start(bf16[32,2,3072]{2,1,0:T(2,128)(2,1)} %reshape.688), calls=%async_computation | async-start | bytes 786432 | tf_op jit(solution)/shard_map/all_to_all | solution.py:152
  137.2 0.1 select_reduce_fusion.4
  137.3 0.1 fusion.51
  137.5 0.1 pad_add_fusion
  137.6 0.1 compare_select_fusion
  137.6 0.1 copy.41
  137.8 0.1 reshape.674
  138.0 0.1 copy.33
  138.1 0.2 fusion.27
  138.3 0.1 broadcast_add_fusion
  138.4 0.2 fusion.30
  138.7 12.7 %all-to-all-done = bf16[32,2,3072]{2,1,0:T(2,128)(2,1)S(1)} async-done(((bf16[32,2,3072]{2,1,0:T(2,128)(2,1)}), bf16[32,2,3072]{2,1,0:T(2,128)(2,1)S(1)}, u32[]{:S(2)}, u32[]{:S(2)}) %all-to-all-start) | async-done | bytes 393248 | tf_op jit(solution)/shard_map/all_to_all | solution.py:152
  151.4 2.0 reshape.689
  153.4 3.3 %bitcast_convert_fusion = f32[1,48,4096]{1,0,2:T(1,128)} fusion(bf16[4096,1,48]{2,1,0:T(2,128)(2,1)S(1)} %reshape.689), kind=kLoop, calls=%fused_computation.148 | loop fusion | flops 196608 | bytes 1179648 | tf_op jit(solution)/shard_map/convert_element_type | solution.py:173
  156.7 2.2 copy.36
  158.9 15.0 %all-gather.5.cloned.1.call-done = bf16[1536,4096]{1,0:T(8,128)(2,1)} async-done(((bf16[1536,128]{1,0:T(8,128)(2,1)}), bf16[1536,4096]{1,0:T(8,128)(2,1)}) %all-gather.5.cloned.1.call-update) | async-done | bytes 12582928 | tf_op jit(solution)/shard_map/all_gather | solution.py:169
  173.8 6.5 %fusion.11 = bf16[1536,128]{1,0:T(8,128)(2,1)S(1)} fusion(f32[1536,128]{1,0:T(8,128)S(1)} %bitcast.86, bf16[1536,4096]{1,0:T(8,128)(2,1)} %all-gather.5.cloned.1.call-done, bf16[4096,128]{1,0:T(8,128)(2,1)S(1)} %copy-done, f32[128]{0:T(128)S(1)} %copy-done.9), kind=kOutput, calls=%fused_computation.18 | convolution fusion | flops 1611202560 | bytes 14811648 | tf_op jit(solution)/shard_map/dot_general | solution.py:168
  180.4 3.2 %gather_fusion = bf16[1536,128]{1,0:T(8,128)(2,1)S(1)} fusion(bf16[1536,128]{1,0:T(8,128)(2,1)S(1)} %fusion.11, s32[2048]{0:T(1024)S(1)} %pad_clamp_fusion), kind=kCustom, calls=%fused_computation | custom fusion | bytes 792576 | tf_op jit(solution)/shard_map/gather | solution.py:176
  183.6 0.2 gather.6
  183.8 6.6 %convolution_convert_fusion = bf16[512,4096]{1,0:T(8,128)(2,1)} fusion(bf16[512,4096]{1,0:T(8,128)(2,1)} %bitcast.93, bf16[384,512]{1,0:T(8,128)(2,1)S(1)} %gather.6, s32[384]{0:T(512)S(1)} %multiply_add_fusion, pred[384]{0:T(512)(128)(4,1)S(1)} %broadcast_compare_fusion), kind=kOutput, calls=%fused_computation.14 | convolution fusion | flops 2351562752 | bytes 8783744 | tf_op jit(solution)/shard_map/dot_general | solution.py:184
  190.5 7.2 %reshape.667 = bf16[128,4,4096]{2,1,0:T(4,128)(2,1)} reshape(bf16[512,4096]{1,0:T(8,128)(2,1)} %convolution_convert_fusion) | data formatting | bytes 8388608 | tf_op jit(solution)/shard_map/reshape | solution.py:187
  197.7 60.7 %all_to_all.14 = bf16[128,4,4096]{2,1,0:T(4,128)(2,1)S(1)} all-to-all(bf16[128,4,4096]{2,1,0:T(4,128)(2,1)} %reshape.667), channel_id=1, replica_groups=mesh['dp'=4,'tensor'=32] {'dp','tensor'}, dimensions={0} | all-to-all | bytes 8388608 | tf_op jit(solution)/shard_map/all_to_all | solution.py:188
  258.3 2.1 bitcast_reduce_fusion
  260.5 0.7 reshape.669
  (42 shorter events, 0.3 us)
Async XLA Ops:
  6.5 167.3 %copy-start = (bf16[4096,128]{1,0:T(8,128)(2,1)S(1)}, bf16[4096,128]{1,0:T(8,128)(2,1)}, u32[]{:S(2)}) copy-start(bf16[4096,128]{1,0:T(8,128)(2,1)} %param.16) | copy-start | bytes 3145732
  6.5 71.0 %all-gather.3.cloned.1.call-start = ((), (), s32[]{:S(2)}) async-start(), calls=%async_computation.2 | async-start | bytes 12976128 | tf_op jit(solution)/shard_map/all_gather | solution.py:136
  11.1 162.7 %all-gather.5.cloned.1.call-start = ((), (), s32[]{:S(2)}) async-start(), calls=%async_computation.3 | async-start | bytes 12976128 | tf_op jit(solution)/shard_map/all_gather | solution.py:169
  12.1 5.6 %copy-start.5 = (s32[3,1]{0,1:T(1,128)}, s32[3,1]{0,1:T(1,128)S(1)}, u32[]{:S(2)}) copy-start(s32[3,1]{0,1:T(1,128)S(1)} %reduce-window.27) | copy-start | bytes 40
  13.0 4.8 %copy-start.4 = (s32[1,3,2]{1,2,0:T(2,128)S(1)}, s32[1,3,2]{1,2,0:T(2,128)}, u32[]{:S(2)}) copy-start(s32[1,3,2]{1,2,0:T(2,128)} %param.20) | copy-start | bytes 76
  86.7 2.4 copy-start.3
  89.1 11.9 %copy-start.1 = (bf16[1,48,4096]{2,1,0:T(8,128)(2,1)S(1)}, bf16[1,48,4096]{2,1,0:T(8,128)(2,1)}, u32[]{:S(2)}) copy-start(bf16[1,48,4096]{2,1,0:T(8,128)(2,1)} %param.12) | copy-start | bytes 1179652
  100.2 0.8 copy-start.2
  103.8 33.4 %copy-start.6 = (s32[3,1]{0,1:T(1,128)S(1)}, s32[3,1]{0,1:T(1,128)}, u32[]{:S(2)}) copy-start(s32[3,1]{0,1:T(1,128)} %copy-done.5) | copy-start | bytes 40
  103.8 33.4 %copy-start.7 = (s32[3]{0:T(128)S(1)}, s32[3]{0:T(128)}, u32[]{:S(2)}) copy-start(s32[3]{0:T(128)} %get-tuple-element.118) | copy-start | bytes 40
  103.8 34.1 %copy-start.8 = (s32[1,384,1]{1,2,0:T(1,128)S(1)}, s32[1,384,1]{1,2,0:T(1,128)}, u32[]{:S(2)}) copy-start(s32[1,384,1]{1,2,0:T(1,128)} %param.21) | copy-start | bytes 4612
  131.7 19.6 %all-to-all-start = ((bf16[32,2,3072]{2,1,0:T(2,128)(2,1)}), bf16[32,2,3072]{2,1,0:T(2,128)(2,1)S(1)}, u32[]{:S(2)}, u32[]{:S(2)}) async-start(bf16[32,2,3072]{2,1,0:T(2,128)(2,1)} %reshape.688), calls=%async_computation | async-start | bytes 786432 | tf_op jit(solution)/shard_map/all_to_all | solution.py:152
  153.4 20.5 %copy-start.9 = (f32[128]{0:T(128)S(1)}, f32[128]{0:T(128)}, u32[]{:S(2)}) copy-start(f32[128]{0:T(128)} %param.17) | copy-start | bytes 1540
Sparse Core Ops, SparseCore 0:
  11.2 66.2 all-gather.2
  101.1 72.7 all-gather.4
where the time goes:
time: 269 us; the launch traced here: 268 us
  waiting for transfers between devices  86.6 us (32%)
  blocking collectives  60.7 us (23%)
  other arithmetic  40.9 us (15%)
  local copies, waits for them, and re-layouts  31.4 us (12%)
  matrix products  27.1 us (10%)
  between operations  13.8 us (5%)
  starting transfers between devices  5.48 us (2%)
    all_to_all x1, blocking collectives, local(): lax.all_to_all(outgoing, ('dp', 'tensor'), split_axis=0, concat_axis=0, t...  60.7 us
    all_gather x1, waiting for transfers between devices, local(): normed = lax.all_gather(normed_local, 'tensor', axis=1, tiled=True)[0]  58.9 us
    unnamed x3, other arithmetic  24.4 us
    all_gather x1, waiting for transfers between devices, local(): lax.all_gather(head_outputs, 'tensor', axis=1, tiled=True)  15 us
    unnamed x25, local copies, waits for them, and re-layouts  14.6 us
    all_to_all x1, waiting for transfers between devices, local(): lax.all_to_all(tokens, 'tensor', split_axis=2, concat_axis=1, tiled=True)[0]  12.7 us
    dot_general x1, matrix products, local(): product = jnp.dot(normed, qkv_weight, preferred_element_type=jnp.float32)  9.01 us
    reshape x1, local copies, waits for them, and re-layouts, local(): outgoing = group_part.reshape(device_count, own_cap, out_width)  7.19 us
  transfers between devices with their start and end apart: 3, of which 3 were waited for; matrix products, arithmetic and copies ran while one was open for 18% of the time, Pallas kernels for 0%

commit v1 on v0

v1 whole, which is shorter than its diff:
```python
import jax
import jax.numpy as jnp
from jax import lax
from jax.sharding import Mesh
from jax.sharding import PartitionSpec as P

HEAD_DIM = 128
IMGS = 3
REG = 5


norm_eps = 1e-06


def layer_norm(row_data, gain_vec, shift_vec):
    values = row_data.astype(jnp.float32)
    center = values - jnp.mean(values, axis=-1, keepdims=True)
    spread = jnp.mean(center * center, axis=-1, keepdims=True)
    return (center * lax.rsqrt(spread + norm_eps) * gain_vec + shift_vec).astype(jnp.bfloat16)


def image_layout(grid_row):
    heights = grid_row[:, 0]
    widths = grid_row[:, 1]
    lengths = REG + heights * widths
    starts = jnp.cumsum(lengths) - lengths
    counts = heights // 2 * (widths // 2)
    merged_end = jnp.cumsum(counts)
    return (heights, widths, starts, merged_end - counts, merged_end)


def pick_rows(onehot, lookup):
    return jnp.sum(onehot * lookup[None, :], axis=1)


def rope_tables(seg_at, position, grid_row):
    heights, widths, starts, first_merged, last_merged = image_layout(grid_row)
    image_ids = jnp.arange(IMGS, dtype=jnp.int32)
    onehot = (seg_at[:, None] == image_ids[None, :]).astype(jnp.int32)
    is_image = jnp.sum(onehot, axis=1) > 0
    in_image = position - pick_rows(onehot, starts) - REG
    is_patch = is_image & (in_image >= 0)
    row_width = jnp.maximum(pick_rows(onehot, widths), 1)
    col_height = jnp.maximum(pick_rows(onehot, heights), 1)
    clipped = jnp.maximum(in_image, 0)
    coord_y = (
        2.0 * ((clipped // row_width).astype(jnp.float32) + 0.5) / col_height.astype(jnp.float32)
        - 1.0
    )
    coord_x = (
        2.0 * ((clipped % row_width).astype(jnp.float32) + 0.5) / row_width.astype(jnp.float32)
        - 1.0
    )
    quarter = HEAD_DIM // 4
    pair_ids = jnp.arange(HEAD_DIM // 2, dtype=jnp.int32)
    omegas = 100.0 ** ((pair_ids % quarter).astype(jnp.float32) / quarter)
    coord_all = jnp.where(pair_ids[None, :] < quarter, coord_y[:, None], coord_x[:, None])
    angles = jnp.where(is_patch[:, None], jnp.pi * omegas[None, :] * coord_all, 0.0)
    return (jnp.cos(angles), jnp.sin(angles))


def rotate(values, cos_rows, sin_rows):
    half_dim = values.shape[-1] // 2
    first_half = values[..., :half_dim]
    second_half = values[..., half_dim:]
    return jnp.concatenate(
        [
            first_half * cos_rows - second_half * sin_rows,
            second_half * cos_rows + first_half * sin_rows,
        ],
        axis=-1,
    )


def merge_sources(grid_row, merged_rows):
    heights, widths, starts, first_merged, last_merged = image_layout(grid_row)
    row_ids = jnp.arange(merged_rows, dtype=jnp.int32)
    onehot = (
        (row_ids[:, None] >= first_merged[None, :]) & (row_ids[:, None] < last_merged[None, :])
    ).astype(jnp.int32)
    is_valid = jnp.sum(onehot, axis=1) > 0
    row_width = pick_rows(onehot, widths)
    half_width = jnp.maximum(row_width // 2, 1)
    in_image = row_ids - pick_rows(onehot, first_merged)
    corner = (
        pick_rows(onehot, starts)
        + REG
        + 2 * (in_image // half_width) * row_width
        + 2 * (in_image % half_width)
    )
    offsets = jnp.stack(
        [jnp.zeros_like(row_width), jnp.ones_like(row_width), row_width, row_width + 1], axis=1
    )
    sources = jnp.where(is_valid[:, None], corner[:, None] + offsets, 0)
    return (sources, is_valid)


def attend(query_rows, query_seg, key_rows, value_rows, key_seg):
    scores = lax.dot_general(
        query_rows, key_rows, (((1,), (1,)), ((), ())), preferred_element_type=jnp.float32
    ) * HEAD_DIM ** (-0.5)
    scores = jnp.where(query_seg[:, None] == key_seg[None, :], scores, -jnp.inf)
    shifted = jnp.exp(scores - jnp.max(scores, axis=1, keepdims=True))
    weights = (shifted / jnp.sum(shifted, axis=1, keepdims=True)).astype(jnp.bfloat16)
    return jnp.dot(weights, value_rows, preferred_element_type=jnp.float32).astype(jnp.bfloat16)


def owner_ranks(owner_row):
    rows = owner_row.shape[0]
    same = owner_row[:, None] == owner_row[None, :]
    earlier = jnp.arange(rows)[None, :] < jnp.arange(rows)[:, None]
    return jnp.sum((same & earlier).astype(jnp.int32), axis=1)


def local(
    tokens, ln_gain, ln_bias, w_qkv, w_out, layer_scale, w_merge, segment_ids, grid_sizes, owners
):
    chips = lax.axis_size("xy")
    batch_count = lax.axis_size("dp")
    chip = lax.axis_index("xy")
    core = lax.axis_index("core")
    seg_row = segment_ids[0]
    grid_row = grid_sizes[0]
    owner_row = owners[0, :, 0]
    seq_len = seg_row.shape[0]
    block = tokens.shape[1]
    model_width = tokens.shape[2]
    col_width = layer_scale.shape[0]
    half_rows = chips * block
    merged_rows = seq_len // 4
    tensor_count = 2 * chips
    own_cap = 4
    out_width = w_merge.shape[2]

    x_rows = lax.all_gather(tokens[0], "xy", axis=0, tiled=True)
    w_pair = lax.all_gather(w_qkv, "core", axis=0, tiled=False)
    wo_pair = lax.all_gather(w_out, "core", axis=0, tiled=False)
    ls_pair = lax.all_gather(layer_scale, "core", axis=0, tiled=True)

    position = (
        (2 * jnp.arange(chips, dtype=jnp.int32) + core)[:, None] * block
        + jnp.arange(block, dtype=jnp.int32)[None, :]
    ).reshape(half_rows)
    seg_mine = seg_row.reshape(chips, 2, block)
    seg_both = jnp.transpose(seg_mine, (1, 0, 2)).reshape(2, half_rows)
    seg_here = seg_both[core]
    cos_t, sin_t = rope_tables(seg_here, position, grid_row)

    normed = layer_norm(x_rows, ln_gain, ln_bias)
    qkv_weight = jnp.transpose(w_pair, (1, 2, 0, 3)).reshape(model_width, 3 * 2 * HEAD_DIM)
    product = jnp.dot(normed, qkv_weight, preferred_element_type=jnp.float32).reshape(
        half_rows, 3, 2, HEAD_DIM
    )
    cos_rows = cos_t[:, None, :]
    sin_rows = sin_t[:, None, :]
    q_here = rotate(product[:, 0], cos_rows, sin_rows).astype(jnp.bfloat16)
    k_here = rotate(product[:, 1], cos_rows, sin_rows).astype(jnp.bfloat16)
    v_here = product[:, 2].astype(jnp.bfloat16)
    kv_here = jnp.stack([k_here, v_here], axis=1)
    kv_all = lax.all_gather(kv_here, "core", axis=0, tiled=True)
    key_all = kv_all[:, 0]
    value_all = kv_all[:, 1]
    seg_keys = seg_both.reshape(2 * half_rows)

    def one_head(h):
        return attend(q_here[:, h], seg_here, key_all[:, h], value_all[:, h], seg_keys)

    context_here = jnp.stack([one_head(0), one_head(1)], axis=1).reshape(
        half_rows, 2 * HEAD_DIM
    )
    context_g = lax.all_gather(context_here, "xy", axis=0, tiled=False)
    context = jnp.transpose(context_g, (1, 0, 2)).reshape(half_rows, model_width)
    wo_cols = jnp.transpose(wo_pair, (1, 0, 2)).reshape(model_width, 2 * col_width)
    mixed = jnp.dot(context, wo_cols, preferred_element_type=jnp.float32)
    x_cols = lax.dynamic_slice_in_dim(x_rows, chip * 2 * col_width, 2 * col_width, 1)
    hidden_here = (x_cols.astype(jnp.float32) + ls_pair * mixed).astype(jnp.bfloat16)
    hidden_sw = lax.all_to_all(
        hidden_here.reshape(half_rows, 2, col_width), "core", split_axis=1, concat_axis=1
    )
    hidden = jnp.transpose(
        hidden_sw.reshape(chips, block, 2, col_width), (0, 2, 1, 3)
    ).reshape(seq_len, col_width)

    sources, is_valid = merge_sources(grid_row, merged_rows)
    merged = jnp.where(
        is_valid[:, None, None], hidden[sources], jnp.zeros((), jnp.bfloat16)
    ).reshape(merged_rows, 4 * col_width)
    merge_weight = w_merge.reshape(4 * col_width, out_width)
    ranks = owner_ranks(owner_row)
    owner_dp = owner_row // tensor_count
    owner_t = owner_row % tensor_count
    slot_block = (owner_t % 2) * chips + owner_t // 2
    slot_keys = slot_block * (batch_count * own_cap) + owner_dp * own_cap + ranks
    slot_ids = jnp.arange(tensor_count * batch_count * own_cap, dtype=jnp.int32)
    placing = (slot_ids[:, None] == slot_keys[None, :]).astype(jnp.bfloat16)
    by_owner = jnp.dot(placing, merged, preferred_element_type=jnp.float32).astype(jnp.bfloat16)
    group_part = jnp.dot(by_owner, merge_weight, preferred_element_type=jnp.float32).astype(
        jnp.bfloat16
    )
    part32 = group_part.astype(jnp.float32)
    half = lax.psum_scatter(part32, "core", scatter_dimension=0, tiled=True)
    mine = lax.psum_scatter(half, "xy", scatter_dimension=0, tiled=True)
    outgoing = mine.astype(jnp.bfloat16).reshape(batch_count, own_cap, out_width)
    incoming = lax.all_to_all(outgoing, "dp", split_axis=0, concat_axis=0, tiled=True)
    return incoming.reshape(1, batch_count * own_cap, out_width)


def solution(mesh):
    devices = mesh.devices.reshape(mesh.shape["dp"], -1, 2)
    mesh3 = Mesh(devices, ("dp", "xy", "core"))
    tp = ("xy", "core")
    in_specs = (
        P("dp", tp, None),
        P(),
        P(),
        P(None, None, tp),
        P(None, tp),
        P(tp),
        P(None, tp, None),
        P("dp", None),
        P("dp", None, None),
        P("dp", None, None),
    )
    out_specs = P("dp", tp, None)
    return jax.shard_map(local, mesh=mesh3, in_specs=in_specs, out_specs=out_specs, check_vma=False)
```

time: 269 us -> 353 us (1.31)
  waiting for transfers between devices: 86.6 us -> 254 us
  blocking collectives: 60.7 us -> 15.1 us
  other arithmetic: 40.9 us -> 13.7 us
  starting transfers between devices: 5.48 us -> 0.42 us
  matrix products: 27.1 us -> 22.4 us
    reduce_scatter x0 -> x2, waiting for transfers between devices: none -> 100 us  [the longest x1 81 us: local(): mine = lax.psum_scatter(half, 'xy', scatter_dimension=0, tiled=True)]
    all_gather x2 -> x5, waiting for transfers between devices: 73.9 us -> 152 us  [the longest x1 59.8 us: local(): context_g = lax.all_gather(context_here, 'xy', axis=0, tiled=False)]
    all_to_all x1 -> x2, blocking collectives: 60.7 us -> 13.3 us  [the longest x1 8.76 us: local(): lax.all_to_all(outgoing, 'dp', split_axis=0, concat_axis=0, tiled=True)]
    unnamed x3 -> x2, other arithmetic: 24.4 us -> 0.74 us
    unnamed x25 -> x13, local copies, waits for them, and re-layouts: 14.6 us -> 1.17 us
    all_to_all x1 -> x0, waiting for transfers between devices: 12.7 us -> none  [local(): lax.all_to_all(tokens, 'tensor', split_axis=2, concat_axis=1, tiled=True)[0]]
    transpose x0 -> x3, local copies, waits for them, and re-layouts: none -> 11.6 us  [the longest x1 8.69 us: local(): jnp.transpose(w_pair, (1, 2, 0, 3)).reshape(model_width, 3 * 2 * HEAD_DIM)]
    all_gather x0 -> x1, local copies, waits for them, and re-layouts: none -> 8.67 us  [local(): context_g = lax.all_gather(context_here, 'xy', axis=0, tiled=False)]
  transfers between devices with their start and end apart: 3 -> 7, of which waited for: 3 -> 7; matrix products, arithmetic and copies ran while one was open for 18% -> 7% of each run, Pallas kernels for 0% -> 0%
where the time goes in v1:
time: 353 us; the launch traced here: 350 us
  waiting for transfers between devices  254 us (72%)
  local copies, waits for them, and re-layouts  30.1 us (9%)
  matrix products  22.4 us (6%)
  blocking collectives  15.1 us (4%)
  between operations  13.8 us (4%)
  other arithmetic  13.7 us (4%)
    reduce_scatter x1, waiting for transfers between devices, local(): mine = lax.psum_scatter(half, 'xy', scatter_dimension=0, tiled=True)  81 us
    all_gather x1, waiting for transfers between devices, local(): context_g = lax.all_gather(context_here, 'xy', axis=0, tiled=False)  59.8 us
    all_gather x1, waiting for transfers between devices, local(): x_rows = lax.all_gather(tokens[0], 'xy', axis=0, tiled=True)  55.4 us
    all_gather x1, waiting for transfers between devices, local(): w_pair = lax.all_gather(w_qkv, 'core', axis=0, tiled=False)  20 us
    reduce_scatter x1, waiting for transfers between devices, local(): half = lax.psum_scatter(part32, 'core', scatter_dimension=0, tiled=True)  19 us
    all_gather x1, waiting for transfers between devices, local(): kv_all = lax.all_gather(kv_here, 'core', axis=0, tiled=True)  12.1 us
    all_to_all x1, blocking collectives, local(): lax.all_to_all(outgoing, 'dp', split_axis=0, concat_axis=0, tiled=True)  8.76 us
    transpose x1, local copies, waits for them, and re-layouts, local(): jnp.transpose(w_pair, (1, 2, 0, 3)).reshape(model_width, 3 * 2 * HEAD_DIM)  8.69 us
  transfers between devices with their start and end apart: 7, of which 7 were waited for; matrix products, arithmetic and copies ran while one was open for 7% of the time, Pallas kernels for 0%

profile of v1, /device:TPU:1, one launch (start us, length us, event | category | flops | bytes accessed | tf_op | source)
XLA Modules:
  0.0 349.8 jit_solution(11799699220335604233)
XLA Ops:
  6.5 0.7 all-gather.16.cloned.1.call-update
  7.3 0.7 all-gather.14.cloned.1.call-update
  8.1 0.8 fusion.79
  8.8 0.2 reduce-window.15
  9.0 0.2 reduce-window.16
  9.2 0.1 iota_add_fusion
  9.3 0.1 add.306
  9.3 0.7 reduce.2
  10.1 0.1 reshape_squeeze.3
  10.2 0.1 reshape.661
  10.3 0.8 multiply_subtract_fusion
  11.1 0.1 convert_reduce_fusion.2
  11.2 0.1 fusion.49
  11.3 0.8 fusion.43
  12.1 20.0 %all-gather.16.cloned.1.call-done = bf16[8192,3,128]{2,0,1:T(8,128)(2,1)} async-done(((bf16[4096,3,128]{2,0,1:T(8,128)(2,1)}), bf16[8192,3,128]{2,0,1:T(8,128)(2,1)}) %all-gather.16.cloned.1.call-update) | async-done | bytes 6291472 | tf_op jit(solution)/shard_map/all_gather | solution.py:136
  32.1 8.7 %copy.49 = bf16[4096,3,2,128]{0,3,2,1:T(8,128)(2,1)} copy(bf16[4096,3,2,128]{3,0,2,1:T(8,128)(2,1)} %bitcast.123) | data formatting | bytes 12582912 | tf_op jit(solution)/shard_map/transpose | solution.py:150
  40.8 55.4 %all-gather.14.cloned.1.call-done = bf16[1,768,4096]{2,1,0:T(8,128)(2,1)} async-done(((bf16[1,48,4096]{2,1,0:T(8,128)(2,1)}), bf16[1,768,4096]{2,1,0:T(8,128)(2,1)}) %all-gather.14.cloned.1.call-update) | async-done | bytes 6291472 | tf_op jit(solution)/shard_map/all_gather | solution.py:135
  96.2 3.8 %convert_reduce_fusion = f32[768]{0:T(1024)S(1)} fusion(bf16[1,768,4096]{2,1,0:T(8,128)(2,1)} %all-gather.14.cloned.1.call-done), kind=kLoop, calls=%fused_computation.1 | loop fusion | flops 6290688 | bytes 6294528 | tf_op jit(solution)/shard_map/reduce_sum | solution.py:17
  100.1 0.7 copy-done
  100.8 1.8 fusion.3
  102.6 0.2 copy-done.1
  102.8 5.4 %fusion.8 = f32[768,3,2,128]{0,3,2,1:T(8,128)S(1)} fusion(bf16[4096,3,2,128]{0,3,2,1:T(8,128)(2,1)S(1)} %copy-done.1, bf16[1,768,4096]{2,1,0:T(8,128)(2,1)S(1)} %copy-done, f32[4096]{0:T(1024)S(1)} %copy-done.3, f32[4096]{0:T(1024)S(1)} %copy-done.4, f32[768]{0:T(1024)S(1)} %add_rsqrt_fusion, f32[768]{0:T(1024)S(1)} %broadcast_multiply_fusion), kind=kOutput, calls=%fused_computation.11 | convolution fusion | flops 4850712576 | bytes 14981120 | tf_op jit(solution)/shard_map/dot_general | solution.py:151
  108.3 0.1 slice_bitcast_fusion.3
  108.4 0.2 subtract_convert_fusion.1
  108.7 1.0 pad_maximum_fusion
  109.7 0.5 all-gather.18.cloned.1.call-update
  110.3 0.2 all-gather.12.cloned.1.call-start
  110.5 0.1 eq.92
  110.6 12.1 %all-gather.10.cloned.1.call-done = bf16[1536,2,2,128]{0,3,2,1:T(8,128)(2,1)} async-done(((bf16[768,2,2,128]{0,3,2,1:T(8,128)(2,1)}), bf16[1536,2,2,128]{0,3,2,1:T(8,128)(2,1)}) %all-gather.10.cloned.1.call-update) | async-done | bytes 1572880 | tf_op jit(solution)/shard_map/all_gather | solution.py:160
  122.7 1.5 slice_bitcast_fusion
  124.1 0.9 fusion.84
  125.1 0.9 fusion.85
  126.0 0.8 fusion.16
  126.8 0.8 fusion.15
  127.6 1.2 fusion.24
  128.8 1.2 fusion.23
  130.0 1.0 copy.50
  131.0 0.0 reduce-scatter.3.cloned.1.call-start
  131.1 0.1 select_reduce_fusion.4
  131.2 0.1 fusion.67
  131.4 0.1 pad_add_fusion
  131.4 0.1 compare_select_fusion.2
  131.5 0.1 copy.55
  131.7 0.1 reshape.674
  131.8 1.8 all-gather.3
  133.7 0.2 convert_reduce_fusion.1
  133.9 4.9 %all-gather.18.cloned.1.call-done = bf16[8192,128]{1,0:T(8,128)(2,1)} async-done(((bf16[4096,128]{1,0:T(8,128)(2,1)}), bf16[8192,128]{1,0:T(8,128)(2,1)}) %all-gather.18.cloned.1.call-update) | async-done | bytes 2097168 | tf_op jit(solution)/shard_map/all_gather | solution.py:137
  138.8 2.9 copy.52
  141.8 1.0 constant_dynamic-slice_fusion
  142.8 0.2 copy.57
  143.0 59.8 %all-gather.12.cloned.1.call-done = bf16[16,768,256]{2,1,0:T(8,128)(2,1)} async-done(((bf16[1,768,256]{2,1,0:T(8,128)(2,1)}), bf16[16,768,256]{2,1,0:T(8,128)(2,1)}) %all-gather.12.cloned.1.call-update) | async-done | bytes 6291472 | tf_op jit(solution)/shard_map/all_gather | solution.py:171
  202.8 8.7 %copy.51 = bf16[16,768,256]{1,2,0:T(8,128)(2,1)} copy(bf16[16,768,256]{2,1,0:T(8,128)(2,1)} %all-gather.12.cloned.1.call-done) | data formatting | bytes 12582912 | tf_op jit(solution)/shard_map/all_gather | solution.py:171
  211.5 4.6 %fusion.20 = bf16[768,256]{0,1:T(8,128)(2,1)S(1)} fusion(bf16[4096,256]{0,1:T(8,128)(2,1)S(1)} %bitcast.127, bf16[768,4096]{0,1:T(8,128)(2,1)} %bitcast.124, bf16[1,768,256]{1,2,0:T(8,128)(2,1)S(1)} %copy.57, f32[256]{0:T(256)S(1)} %bitcast.137), kind=kOutput, calls=%fused_computation.31 | convolution fusion | flops 1611399168 | bytes 9176064 | tf_op jit(solution)/shard_map/dot_general | solution.py:174
  216.1 0.2 copy.53
  216.3 4.5 %all_to_all.10 = bf16[768,2,128]{2,0,1:T(8,128)(2,1)S(1)} all-to-all(bf16[768,2,128]{2,0,1:T(8,128)(2,1)S(1)} %copy.53), channel_id=1, replica_groups=mesh['dp'=4,'xy'=16,'core'=2] {'core'}, dimensions={1} | all-to-all | bytes 786432 | tf_op jit(solution)/shard_map/all_to_all | solution.py:177
  220.9 3.2 gather_fusion
  224.1 0.2 gather.6
  224.3 8.1 %fusion.14 = f32[512,4096]{1,0:T(8,128)} fusion(bf16[512,4096]{1,0:T(8,128)(2,1)} %bitcast.125, bf16[384,512]{1,0:T(8,128)(2,1)S(1)} %gather.6, s32[384]{0:T(512)S(1)} %fusion.60, pred[384]{0:T(512)(128)(4,1)S(1)} %broadcast_compare_fusion), kind=kOutput, calls=%fused_computation.17 | convolution fusion | flops 2353659904 | bytes 12978048 | tf_op jit(solution)/shard_map/dot_general | solution.py:197
  232.5 19.0 %reduce-scatter.3.cloned.1.call-done = f32[256,4096]{1,0:T(8,128)} async-done(((f32[512,4096]{1,0:T(8,128)}), f32[256,4096]{1,0:T(8,128)}) %reduce-scatter.3.cloned.1.call-update) | async-done | bytes 4194320 | tf_op jit(solution)/shard_map/reduce_scatter | solution.py:201
  251.5 81.0 %reduce-scatter.5.cloned.1.call-done = f32[16,4096]{1,0:T(8,128)} async-done(((f32[256,4096]{1,0:T(8,128)}), f32[16,4096]{1,0:T(8,128)}) %reduce-scatter.5.cloned.1.call-update) | async-done | bytes 262160 | tf_op jit(solution)/shard_map/reduce_scatter | solution.py:202
  332.5 1.0 convert_element_type.111
  333.5 0.1 reshape.670
  333.5 8.8 %all_to_all.11 = bf16[4,4,4096]{2,1,0:T(4,128)(2,1)S(1)} all-to-all(bf16[4,4,4096]{2,1,0:T(4,128)(2,1)S(1)} %reshape.670), channel_id=1, replica_groups=mesh['dp'=4,'xy'=16,'core'=2] {'dp'}, dimensions={0} | all-to-all | bytes 262144 | tf_op jit(solution)/shard_map/all_to_all | solution.py:204
  342.3 0.7 reshape.671
  (36 shorter events, 0.5 us)
Async XLA Ops:
  6.5 25.6 %all-gather.16.cloned.1.call-start = ((), (), s32[]{:S(2)}) async-start(), calls=%async_computation.9 | async-start | bytes 9437184 | tf_op jit(solution)/shard_map/all_gather | solution.py:136
  7.3 89.0 %all-gather.14.cloned.1.call-start = ((), (), s32[]{:S(2)}) async-start(), calls=%async_computation.8 | async-start | bytes 6684672 | tf_op jit(solution)/shard_map/all_gather | solution.py:135
  8.0 114.7 %all-gather.10.cloned.1.call-start = ((), (), s32[]{:S(2)}) async-start(), calls=%async_computation.4 | async-start | bytes 2359296 | tf_op jit(solution)/shard_map/all_gather | solution.py:160
  32.1 70.5 %copy-start.4 = (f32[4096]{0:T(1024)S(1)}, f32[4096]{0:T(1024)}, u32[]{:S(2)}) copy-start(f32[4096]{0:T(1024)} %param.11) | copy-start | bytes 49156
  96.2 4.6 %copy-start = (bf16[1,768,4096]{2,1,0:T(8,128)(2,1)S(1)}, bf16[1,768,4096]{2,1,0:T(8,128)(2,1)}, u32[]{:S(2)}) copy-start(bf16[1,768,4096]{2,1,0:T(8,128)(2,1)} %all-gather.14.cloned.1.call-done) | copy-start | bytes 18874372
  100.0 2.8 copy-start.1
  100.0 2.8 copy-start.3
  109.7 29.2 %all-gather.18.cloned.1.call-start = ((), (), s32[]{:S(2)}) async-start(), calls=%async_computation.10 | async-start | bytes 3145728 | tf_op jit(solution)/shard_map/all_gather | solution.py:137
  110.3 92.5 %all-gather.12.cloned.1.call-start = ((), (), s32[]{:S(2)}) async-start(), calls=%async_computation.5 | async-start | bytes 6684672 | tf_op jit(solution)/shard_map/all_gather | solution.py:171
  128.8 2.3 copy-start.2
  128.8 3.0 copy-start.5
  131.0 120.5 %reduce-scatter.3.cloned.1.call-start = ((), (), s32[]{:S(2)}) async-start(), calls=%async_computation.6 | async-start | bytes 12582912 | tf_op jit(solution)/shard_map/reduce_scatter | solution.py:201
  232.5 100.0 %reduce-scatter.5.cloned.1.call-start = ((), (), s32[]{:S(2)}) async-start(), calls=%async_computation.7 | async-start | bytes 4456448 | tf_op jit(solution)/shard_map/reduce_scatter | solution.py:202
Sparse Core Ops, SparseCore 0:
  9.0 23.0 all-gather.15
  34.3 61.8 all-gather.13
  109.8 12.8 all-gather.9
  124.2 14.6 all-gather.17
  140.9 61.8 all-gather.11
  232.6 18.8 reduce-scatter.2
  254.8 77.6 reduce-scatter.4
